TPU v7x, 32 devices: a whole 2x2x4 slice. The times are simulated.
32 devices in a mesh: inl: 4 (over y, core), xl: 2 (over x), gz: 4 (over z).
Axes of the slice: x: 2, y: 2, z: 4, core: 2. Of those that a mesh axis runs over, the one named last changes fastest.
Arguments:
- wave_p: float32 [32, 32, 256], P('gz', 'inl', 'xl'), may hold values from -6 to 6
- wave_p_old: float32 [32, 32, 256], P('gz', 'inl', 'xl'), may hold values from -6 to 6
- wave_q: float32 [32, 32, 256], P('gz', 'inl', 'xl'), may hold values from -6 to 6
- wave_q_old: float32 [32, 32, 256], P('gz', 'inl', 'xl'), may hold values from -6 to 6
- courant_square: float32 [32, 32, 256], P('gz', 'inl', 'xl'), may hold values from 0.05 to 0.11
- thomsen_epsilon: float32 [32, 32, 256], P('gz', 'inl', 'xl'), may hold values from 0.1 to 0.35
- thomsen_delta: float32 [32, 32, 256], P('gz', 'inl', 'xl'), may hold values from 0.02 to 0.2
- tilt_angle: float32 [32, 32, 256], P('gz', 'inl', 'xl'), may hold values from -3.140625 to 3.140625
- azimuth: float32 [32, 32, 256], P('gz', 'inl', 'xl'), may hold values from -3.140625 to 3.140625
- shear_ratio: float32 [32, 32, 256], P('gz', 'inl', 'xl'), may hold values from 0.1 to 0.6
- damping: float32 [32, 32, 256], P('gz', 'inl', 'xl'), may hold values from 0 to 0.3
- trace_samples: float32 [8192, 256], P(('inl', 'xl', 'gz')), may hold values from -6 to 6
- resample_filter: float32 [2, 256], replicated, may hold values from -0.375 to 0.375
- line_gain: float32 [64], replicated, may hold values from 0.5 to 4
- receiver_inline: int32 [8192], P(('inl', 'xl', 'gz')), may hold values from 0 to 31, as said below
- receiver_crossline: int32 [8192], P(('inl', 'xl', 'gz')), may hold values from 0 to 255, as said below
- shot_line: int32 [8192], P(('inl', 'xl', 'gz')), may hold values from 0 to 63
Outputs:
- next_p: float32 [32, 32, 256], P('gz', 'inl', 'xl')
- next_q: float32 [32, 32, 256], P('gz', 'inl', 'xl')
- prior_p: float32 [32, 32, 256], P('gz', 'inl', 'xl')
- prior_q: float32 [32, 32, 256], P('gz', 'inl', 'xl')
Inputs may be any that keep to these rules, and one draw needn't show every extreme that they name: In each aligned block of 256 traces (the traces of one device), at most 64 traces lie in one device column (equal receiver_inline // 8 and receiver_crossline // 128); in every block some column holds exactly 64. `receiver_crossline`: see receiver_inline.
All inputs are finite; a program needn't handle non-finite values.
Results may differ from a plain program's by a relative error of at most 0.000075.
Values sent between devices are 32-bit elements; how exact they have to be, the bound alone decides.
No kernel may reach another device: no remote copies, remote signals or barrier semaphores. Data moves between devices by JAX's collectives and lax.ppermute only.
A program may use at most 64 MiB of HBM per device.

v0:
```python
import jax
import jax.numpy as jnp
from jax import lax
from jax.sharding import PartitionSpec as P

second_coef = (-205.0 / 72.0, 8.0 / 5.0, -1.0 / 5.0, 8.0 / 315.0, -1.0 / 560.0)
first_coef = (0.0, 4.0 / 5.0, -1.0 / 5.0, 4.0 / 105.0, -1.0 / 280.0)


def with_halo(block, sides, width):
    for axis, dim in sides:
        count = lax.axis_size(axis)
        forward = [(i, i + 1) for i in range(count - 1)]
        backward = [(target, source) for source, target in forward]
        low = lax.ppermute(
            lax.slice_in_dim(block, block.shape[dim] - width, None, axis=dim), axis, forward
        )
        high = lax.ppermute(lax.slice_in_dim(block, 0, width, axis=dim), axis, backward)
        block = jnp.concatenate([low, block, high], axis=dim)
    return block


def derivatives(padded):
    depth = padded.shape[-3] - 8
    across = padded.shape[-2] - 8
    along = padded.shape[-1] - 8

    def piece(dz, dx, dy):
        return padded[
            ..., 4 + dz : 4 + dz + depth, 4 + dx : 4 + dx + across, 4 + dy : 4 + dy + along
        ]

    center = piece(0, 0, 0)
    u_zz = second_coef[0] * center
    u_xx = second_coef[0] * center
    u_yy = second_coef[0] * center
    for k in range(1, 5):
        u_zz = u_zz + second_coef[k] * (piece(k, 0, 0) + piece(-k, 0, 0))
        u_xx = u_xx + second_coef[k] * (piece(0, k, 0) + piece(0, -k, 0))
        u_yy = u_yy + second_coef[k] * (piece(0, 0, k) + piece(0, 0, -k))
    grad_x = first_coef[1] * (padded[..., :, 5 : 5 + across, :] - padded[..., :, 3 : 3 + across, :])
    grad_y = first_coef[1] * (
        padded[..., :, 4 : 4 + across, 5 : 5 + along]
        - padded[..., :, 4 : 4 + across, 3 : 3 + along]
    )
    for k in range(2, 5):
        grad_x = grad_x + first_coef[k] * (
            padded[..., :, 4 + k : 4 + k + across, :] - padded[..., :, 4 - k : 4 - k + across, :]
        )
        grad_y = grad_y + first_coef[k] * (
            padded[..., :, 4 : 4 + across, 4 + k : 4 + k + along]
            - padded[..., :, 4 : 4 + across, 4 - k : 4 - k + along]
        )
    u_xy = first_coef[1] * (
        grad_x[..., 4 : 4 + depth, :, 5 : 5 + along] - grad_x[..., 4 : 4 + depth, :, 3 : 3 + along]
    )
    u_xz = first_coef[1] * (
        grad_x[..., 5 : 5 + depth, :, 4 : 4 + along] - grad_x[..., 3 : 3 + depth, :, 4 : 4 + along]
    )
    u_yz = first_coef[1] * (grad_y[..., 5 : 5 + depth, :, :] - grad_y[..., 3 : 3 + depth, :, :])
    for k in range(2, 5):
        u_xy = u_xy + first_coef[k] * (
            grad_x[..., 4 : 4 + depth, :, 4 + k : 4 + k + along]
            - grad_x[..., 4 : 4 + depth, :, 4 - k : 4 - k + along]
        )
        u_xz = u_xz + first_coef[k] * (
            grad_x[..., 4 + k : 4 + k + depth, :, 4 : 4 + along]
            - grad_x[..., 4 - k : 4 - k + depth, :, 4 : 4 + along]
        )
        u_yz = u_yz + first_coef[k] * (
            grad_y[..., 4 + k : 4 + k + depth, :, :] - grad_y[..., 4 - k : 4 - k + depth, :, :]
        )
    return (u_zz, u_xx, u_yy, u_xy, u_xz, u_yz)


def anisotropy(tilt_angle, azimuth):
    sin_t = jnp.sin(tilt_angle)
    cos_t = jnp.cos(tilt_angle)
    sin_f = jnp.sin(azimuth)
    cos_f = jnp.cos(azimuth)
    a_xx = sin_t * sin_t * cos_f * cos_f
    a_yy = sin_t * sin_t * sin_f * sin_f
    a_zz = cos_t * cos_t
    a_xy = 2.0 * sin_t * sin_t * sin_f * cos_f
    a_xz = 2.0 * sin_t * cos_t * cos_f
    a_yz = 2.0 * sin_t * cos_t * sin_f
    return (a_xx, a_yy, a_zz, a_xy, a_xz, a_yz)


def advance(padded, current, previous, fields, coefs, plane, top):
    courant, eps_field, delta_field, shear, damp = fields
    a_xx, a_yy, a_zz, a_xy, a_xz, a_yz = coefs
    u_zz, u_xx, u_yy, u_xy, u_xz, u_yz = derivatives(padded)
    h_one = a_xx * u_xx + a_yy * u_yy + a_zz * u_zz + a_xy * u_xy + a_xz * u_xz + a_yz * u_yz
    h_two = u_xx + u_yy + u_zz - h_one
    wave_a = current[0]
    wave_b = current[1]
    old_a = previous[0]
    old_b = previous[1]
    new_a = (
        2.0 * wave_a
        - old_a
        + courant * ((1.0 + 2.0 * eps_field) * h_two[0] + h_one[1] + shear * (h_one[0] - h_one[1]))
        - damp * (wave_a - old_a)
    )
    new_b = (
        2.0 * wave_b
        - old_b
        + courant
        * ((1.0 + 2.0 * delta_field) * h_two[0] + h_one[1] + shear * (h_two[1] - h_two[0]))
        - damp * (wave_b - old_b)
    )
    new_a = new_a.at[top].add(plane)
    new_b = new_b.at[top].add(plane)
    return jnp.stack([new_a, new_b])


def step_amplitudes(samples, resample_filter, line_gain, lines):
    table = jnp.arange(line_gain.shape[0], dtype=jnp.int32)
    gains = jnp.sum(jnp.where(lines[:, None] == table[None, :], line_gain[None, :], 0.0), axis=1)
    return jnp.dot(samples, resample_filter.T, precision=lax.Precision.HIGHEST) * gains[:, None]


def local(
    wave_p,
    wave_p_old,
    wave_q,
    wave_q_old,
    courant_square,
    thomsen_epsilon,
    thomsen_delta,
    tilt_angle,
    azimuth,
    shear_ratio,
    damping,
    trace_samples,
    resample_filter,
    line_gain,
    receiver_inline,
    receiver_crossline,
    shot_line,
):
    depth, inline_cells, cross_cells = wave_p.shape
    cells = inline_cells * cross_cells
    steps = resample_filter.shape[0]
    xl_count = lax.axis_size("xl")
    columns = lax.axis_size("inl") * xl_count
    capacity = 2 * trace_samples.shape[0] // columns
    owner = receiver_inline // inline_cells * xl_count + receiver_crossline // cross_cells
    local_cell = receiver_inline % inline_cells * cross_cells + receiver_crossline % cross_cells
    payload = step_amplitudes(trace_samples, resample_filter, line_gain, shot_line)
    onehot = (owner[:, None] == jnp.arange(columns, dtype=jnp.int32)[None, :]).astype(jnp.int32)
    rank = jnp.sum(jnp.cumsum(onehot, axis=0) * onehot, axis=1) - 1
    slot = owner * capacity + rank
    width = payload.shape[1]
    float_buffer = (
        jnp.zeros((columns * capacity, width), jnp.float32)
        .at[slot]
        .set(payload)
        .reshape(columns, capacity, width)
    )
    label_buffer = (
        jnp.full((columns * capacity,), -1, jnp.int32)
        .at[slot]
        .set(local_cell)
        .reshape(columns, capacity)
    )
    arrived, arrived_labels = (
        lax.all_to_all(float_buffer, ("inl", "xl"), split_axis=0, concat_axis=0, tiled=True),
        lax.all_to_all(label_buffer, ("inl", "xl"), split_axis=0, concat_axis=0, tiled=True),
    )
    amplitude = arrived.reshape(-1, width)
    flat_labels = arrived_labels.reshape(-1)
    target = jnp.where(flat_labels >= 0, flat_labels, cells)
    planes = jnp.zeros((steps, cells), jnp.float32).at[:, target].add(amplitude.T, mode="drop")
    planes = lax.psum(planes, "gz")
    surface_flag = jnp.where(lax.axis_index("gz") == 0, 1.0, 0.0).astype(jnp.float32)
    planes = planes.reshape(steps, inline_cells, cross_cells) * surface_flag
    fields = (courant_square, thomsen_epsilon, thomsen_delta, shear_ratio, damping)
    current = jnp.stack([wave_p, wave_q])
    previous = jnp.stack([wave_p_old, wave_q_old])
    coefs = anisotropy(tilt_angle, azimuth)
    for step in range(steps):
        padded = with_halo(current, (("inl", 2), ("xl", 3), ("gz", 1)), 4)
        newer = advance(padded, current, previous, fields, coefs, planes[step], 0)
        previous = current
        current = newer
    return (current[0], current[1], previous[0], previous[1])


def solution(mesh):
    return jax.shard_map(
        local,
        mesh=mesh,
        in_specs=(
            P("gz", "inl", "xl"),
            P("gz", "inl", "xl"),
            P("gz", "inl", "xl"),
            P("gz", "inl", "xl"),
            P("gz", "inl", "xl"),
            P("gz", "inl", "xl"),
            P("gz", "inl", "xl"),
            P("gz", "inl", "xl"),
            P("gz", "inl", "xl"),
            P("gz", "inl", "xl"),
            P("gz", "inl", "xl"),
            P(("inl", "xl", "gz"), None),
            P(),
            P(),
            P(("inl", "xl", "gz")),
            P(("inl", "xl", "gz")),
            P(("inl", "xl", "gz")),
        ),
        out_specs=(
            P("gz", "inl", "xl"),
            P("gz", "inl", "xl"),
            P("gz", "inl", "xl"),
            P("gz", "inl", "xl"),
        ),
        check_vma=False,
    )
```

profile of v0, /device:TPU:17, one launch (start us, length us, event | category | flops | bytes accessed | tf_op | source)
XLA Modules:
  0.0 108.6 jit_solution(15742423838032627012)
XLA Ops:
  0.6 0.7 fusion.178
  1.4 0.6 reduce-window.6
  2.4 1.4 %scatter_custom_fusion = s32[512]{0:T(512)S(1)} fusion(s32[256]{0:T(256)S(1)} %compare_select_fusion.2, s32[256]{0:T(256)S(1)} %get-tuple-element.96, s32[]{:T(128)} %constant.177.clone.1), kind=kCustom, calls=%fused_computation.335 | custom fusion | bytes 2052 | tf_op jit(solution)/shard_map/scatter | solution.py:165
  3.8 0.7 all_to_all.9
  4.5 4.4 %all-to-all-start = ((s32[8,1,64]{2,1,0:T(1,128)}), s32[8,1,64]{2,1,0:T(1,128)S(1)}, u32[]{:S(2)}, u32[]{:S(2)}) async-start(s32[8,1,64]{2,1,0:T(1,128)} %all_to_all.9), calls=%async_computation | async-start | bytes 8192 | tf_op jit(solution)/shard_map/all_to_all | solution.py:170
  8.9 3.5 %collective-permute-start.1 = (f32[2,8,4,128]{3,2,1,0:T(4,128)S(1)}, f32[2,8,4,128]{3,2,1,0:T(4,128)S(1)}, u32[]{:S(2)}, u32[]{:S(2)}) collective-permute-start(f32[2,8,4,128]{3,2,1,0:T(4,128)S(1)} %get-tuple-element.85), channel_id=1, source_target_pairs={{0,8},{8,16},{16,24},{1,9},{9,17},{17,25},{2,10},{10,18},{18,26},{... | collective-permute-start | bytes 98312 | tf_op jit(solution)/shard_map/ppermute | solution.py:15
  12.5 1.9 %collective-permute-start = (f32[2,8,4,128]{3,2,1,0:T(4,128)S(1)}, f32[2,8,4,128]{3,2,1,0:T(4,128)S(1)}, u32[]{:S(2)}, u32[]{:S(2)}) collective-permute-start(f32[2,8,4,128]{3,2,1,0:T(4,128)S(1)} %get-tuple-element.86), channel_id=1, source_target_pairs={{8,0},{16,8},{24,16},{9,1},{17,9},{25,17},{10,2},{18,10},{26,18},{... | collective-permute-start | bytes 98312 | tf_op jit(solution)/shard_map/ppermute | solution.py:18
  14.5 0.2 fusion.187
  14.8 0.6 copy-done.16
  15.5 0.3 convolution_multiply_fusion
  15.9 1.2 %scatter_custom_fusion.1 = f32[512,2]{1,0:T(8,128)S(1)} fusion(s32[256]{0:T(256)S(1)} %compare_select_fusion.2, f32[256,2]{1,0:T(8,128)S(1)} %copy.28, f32[]{:T(128)} %constant.176.clone.1), kind=kCustom, calls=%fused_computation.67 | custom fusion | bytes 4100 | tf_op jit(solution)/shard_map/scatter | solution.py:159
  17.3 0.7 reshape.234
  18.0 4.3 %all-to-all-start.1 = ((f32[8,1,128]{2,1,0:T(1,128)}), f32[8,1,128]{2,1,0:T(1,128)S(1)}, u32[]{:S(2)}, u32[]{:S(2)}) async-start(f32[8,1,128]{2,1,0:T(1,128)} %reshape.234), calls=%async_computation.1 | async-start | bytes 8192 | tf_op jit(solution)/shard_map/all_to_all | solution.py:169
  22.3 0.5 broadcast.341
  22.8 0.7 reduce.17
  23.6 2.6 %all-to-all-done.1 = f32[8,1,128]{2,1,0:T(1,128)S(1)} async-done(((f32[8,1,128]{2,1,0:T(1,128)}), f32[8,1,128]{2,1,0:T(1,128)S(1)}, u32[]{:S(2)}, u32[]{:S(2)}) %all-to-all-start.1) | async-done | bytes 4128 | tf_op jit(solution)/shard_map/all_to_all | solution.py:169
  26.2 0.5 broadcast.390
  26.7 0.7 reduce.18
  27.6 2.4 %scatter_custom_fusion.2 = f32[2,1024]{0,1:T(8,128)S(1)} fusion(s32[512]{0:T(512)S(1)} %bitcast.139, f32[512,2]{1,0:T(8,128)S(1)} %bitcast.135, f32[]{:T(128)} %constant.176.clone.1), kind=kCustom, calls=%fused_computation.37 | custom fusion | flops 1024 | bytes 8196 | tf_op jit(solution)/shard_map/scatter-add | solution.py:175
  30.0 23.1 %psum.7 = f32[2,1024]{0,1:T(8,128)S(1)} all-reduce(f32[2,1024]{0,1:T(8,128)S(1)} %scatter_custom_fusion.2), channel_id=1, replica_groups=mesh['inl'=4,'xl'=2,'gz'=4] {'gz'}, use_global_device_ids=true, to_apply=%region_7.8 | all-reduce | flops 2048 | bytes 16384 | tf_op jit(solution)/shard_map/psum | solution.py:176
  53.1 0.5 slice_reduce_fusion
  53.8 2.1 %collective-permute-start.3 = (f32[2,8,16,4]{3,2,1,0:T(8,128)S(1)}, f32[2,8,16,4]{3,2,1,0:T(8,128)S(1)}, u32[]{:S(2)}, u32[]{:S(2)}) collective-permute-start(f32[2,8,16,4]{3,2,1,0:T(8,128)S(1)} %get-tuple-element.72), channel_id=1, source_target_pairs={{0,4},{1,5},{2,6},{3,7},{8,12},{9,13},{10,14},{11,15},{16,20},{17,... | collective-permute-start | bytes 12296 | tf_op jit(solution)/shard_map/ppermute | solution.py:15
  55.9 1.3 %collective-permute-start.2 = (f32[2,8,16,4]{3,2,1,0:T(8,128)S(1)}, f32[2,8,16,4]{3,2,1,0:T(8,128)S(1)}, u32[]{:S(2)}, u32[]{:S(2)}) collective-permute-start(f32[2,8,16,4]{3,2,1,0:T(8,128)S(1)} %get-tuple-element.73), channel_id=1, source_target_pairs={{4,0},{5,1},{6,2},{7,3},{12,8},{13,9},{14,10},{15,11},{20,16},{21,... | collective-permute-start | bytes 12296 | tf_op jit(solution)/shard_map/ppermute | solution.py:18
  57.2 0.6 collective-permute-done.3
  57.8 3.8 %collective-permute-done.2 = f32[2,8,16,4]{3,2,1,0:T(8,128)S(1)} collective-permute-done((f32[2,8,16,4]{3,2,1,0:T(8,128)S(1)}, f32[2,8,16,4]{3,2,1,0:T(8,128)S(1)}, u32[]{:S(2)}, u32[]{:S(2)}) %collective-permute-start.2) | collective-permute-done | bytes 4128 | tf_op jit(solution)/shard_map/ppermute | solution.py:18
  61.6 0.2 pad_maximum_fusion.3
  61.9 2.1 %collective-permute-start.4 = (f32[2,4,16,136]{3,2,1,0:T(8,128)S(1)}, f32[2,4,16,136]{3,2,1,0:T(8,128)S(1)}, u32[]{:S(2)}, u32[]{:S(2)}) collective-permute-start(f32[2,4,16,136]{3,2,1,0:T(8,128)S(1)} %get-tuple-element.60), channel_id=1, source_target_pairs={{1,0},{2,1},{3,2},{5,4},{6,5},{7,6},{9,8},{10,9},{11,10},{13,12},{... | collective-permute-start | bytes 208904 | tf_op jit(solution)/shard_map/ppermute | solution.py:18
  63.9 3.2 %collective-permute-start.5 = (f32[2,4,16,136]{3,2,1,0:T(8,128)S(1)}, f32[2,4,16,136]{3,2,1,0:T(8,128)S(1)}, u32[]{:S(2)}, u32[]{:S(2)}) collective-permute-start(f32[2,4,16,136]{3,2,1,0:T(8,128)S(1)} %get-tuple-element.61), channel_id=1, source_target_pairs={{0,1},{1,2},{2,3},{4,5},{5,6},{6,7},{8,9},{9,10},{10,11},{12,13},{... | collective-permute-start | bytes 208904 | tf_op jit(solution)/shard_map/ppermute | solution.py:15
  67.4 0.5 collective-permute-done.4
  67.9 2.3 %collective-permute-done.5 = f32[2,4,16,136]{3,2,1,0:T(8,128)S(1)} collective-permute-done((f32[2,4,16,136]{3,2,1,0:T(8,128)S(1)}, f32[2,4,16,136]{3,2,1,0:T(8,128)S(1)}, u32[]{:S(2)}, u32[]{:S(2)}) %collective-permute-start.5) | collective-permute-done | bytes 69664 | tf_op jit(solution)/shard_map/ppermute | solution.py:15
  70.2 0.2 pad_maximum_fusion
  70.4 0.3 fusion.24
  71.0 0.6 add_subtract_fusion.1
  71.9 10.9 %collective-permute-start.7 = (f32[2,8,4,128]{3,2,1,0:T(4,128)S(1)}, f32[2,8,4,128]{3,2,1,0:T(4,128)S(1)}, u32[]{:S(2)}, u32[]{:S(2)}) collective-permute-start(f32[2,8,4,128]{3,2,1,0:T(4,128)S(1)} %get-tuple-element.76), channel_id=1, source_target_pairs={{0,8},{8,16},{16,24},{1,9},{9,17},{17,25},{2,10},{10,18},{18,26},{... | collective-permute-start | bytes 98312 | tf_op jit(solution)/shard_map/ppermute | solution.py:15
  82.9 1.9 %collective-permute-start.6 = (f32[2,8,4,128]{3,2,1,0:T(4,128)S(1)}, f32[2,8,4,128]{3,2,1,0:T(4,128)S(1)}, u32[]{:S(2)}, u32[]{:S(2)}) collective-permute-start(f32[2,8,4,128]{3,2,1,0:T(4,128)S(1)} %get-tuple-element.77), channel_id=1, source_target_pairs={{8,0},{16,8},{24,16},{9,1},{17,9},{25,17},{10,2},{18,10},{26,18},{... | collective-permute-start | bytes 98312 | tf_op jit(solution)/shard_map/ppermute | solution.py:18
  84.8 3.3 %collective-permute-done.6 = f32[2,8,4,128]{3,2,1,0:T(4,128)S(1)} collective-permute-done((f32[2,8,4,128]{3,2,1,0:T(4,128)S(1)}, f32[2,8,4,128]{3,2,1,0:T(4,128)S(1)}, u32[]{:S(2)}, u32[]{:S(2)}) %collective-permute-start.6) | collective-permute-done | bytes 32800 | tf_op jit(solution)/shard_map/ppermute | solution.py:18
  88.2 1.3 %collective-permute-start.9 = (f32[2,8,16,4]{3,2,1,0:T(8,128)S(1)}, f32[2,8,16,4]{3,2,1,0:T(8,128)S(1)}, u32[]{:S(2)}, u32[]{:S(2)}) collective-permute-start(f32[2,8,16,4]{3,2,1,0:T(8,128)S(1)} %get-tuple-element.68), channel_id=1, source_target_pairs={{0,4},{1,5},{2,6},{3,7},{8,12},{9,13},{10,14},{11,15},{16,20},{17,... | collective-permute-start | bytes 12296 | tf_op jit(solution)/shard_map/ppermute | solution.py:15
  89.5 1.3 %collective-permute-start.8 = (f32[2,8,16,4]{3,2,1,0:T(8,128)S(1)}, f32[2,8,16,4]{3,2,1,0:T(8,128)S(1)}, u32[]{:S(2)}, u32[]{:S(2)}) collective-permute-start(f32[2,8,16,4]{3,2,1,0:T(8,128)S(1)} %get-tuple-element.69), channel_id=1, source_target_pairs={{4,0},{5,1},{6,2},{7,3},{12,8},{13,9},{14,10},{15,11},{20,16},{21,... | collective-permute-start | bytes 12296 | tf_op jit(solution)/shard_map/ppermute | solution.py:18
  90.9 0.6 collective-permute-done.9
  91.4 3.8 %collective-permute-done.8 = f32[2,8,16,4]{3,2,1,0:T(8,128)S(1)} collective-permute-done((f32[2,8,16,4]{3,2,1,0:T(8,128)S(1)}, f32[2,8,16,4]{3,2,1,0:T(8,128)S(1)}, u32[]{:S(2)}, u32[]{:S(2)}) %collective-permute-start.8) | collective-permute-done | bytes 4128 | tf_op jit(solution)/shard_map/ppermute | solution.py:18
  95.5 3.6 %collective-permute-start.10 = (f32[2,4,16,136]{3,2,1,0:T(8,128)S(1)}, f32[2,4,16,136]{3,2,1,0:T(8,128)S(1)}, u32[]{:S(2)}, u32[]{:S(2)}) collective-permute-start(f32[2,4,16,136]{3,2,1,0:T(8,128)S(1)} %get-tuple-element.58), channel_id=1, source_target_pairs={{1,0},{2,1},{3,2},{5,4},{6,5},{7,6},{9,8},{10,9},{11,10},{13,12},{... | collective-permute-start | bytes 208904 | tf_op jit(solution)/shard_map/ppermute | solution.py:18
  99.2 1.9 %collective-permute-start.11 = (f32[2,4,16,136]{3,2,1,0:T(8,128)S(1)}, f32[2,4,16,136]{3,2,1,0:T(8,128)S(1)}, u32[]{:S(2)}, u32[]{:S(2)}) collective-permute-start(f32[2,4,16,136]{3,2,1,0:T(8,128)S(1)} %get-tuple-element.59), channel_id=1, source_target_pairs={{0,1},{1,2},{2,3},{4,5},{5,6},{6,7},{8,9},{9,10},{10,11},{12,13},{... | collective-permute-start | bytes 208904 | tf_op jit(solution)/shard_map/ppermute | solution.py:15
  101.3 1.0 collective-permute-done.10
  102.3 4.2 %collective-permute-done.11 = f32[2,4,16,136]{3,2,1,0:T(8,128)S(1)} collective-permute-done((f32[2,4,16,136]{3,2,1,0:T(8,128)S(1)}, f32[2,4,16,136]{3,2,1,0:T(8,128)S(1)}, u32[]{:S(2)}, u32[]{:S(2)}) %collective-permute-start.11) | collective-permute-done | bytes 69664 | tf_op jit(solution)/shard_map/ppermute | solution.py:15
  106.5 0.2 pad_maximum_fusion.1
  106.7 0.3 fusion.17
  107.3 0.6 add_subtract_fusion
  108.0 0.6 copy-done.10
  (74 shorter events, 2.9 us)
Async XLA Ops:
  0.6 14.2 %copy-start = (f32[256,256]{1,0:T(8,128)S(1)}, f32[256,256]{1,0:T(8,128)}, u32[]{:S(2)}) copy-start(f32[256,256]{1,0:T(8,128)} %param.36) | copy-start | bytes 786436
  1.4 7.4 %copy-start.3 = (f32[8,8,128]{2,1,0:T(8,128)S(1)}, f32[8,8,128]{2,1,0:T(8,128)}, u32[]{:S(2)}) copy-start(f32[8,8,128]{2,1,0:T(8,128)} %param.25) | copy-start | bytes 98308
  1.4 7.4 %copy-start.4 = (f32[8,8,128]{2,1,0:T(8,128)S(1)}, f32[8,8,128]{2,1,0:T(8,128)}, u32[]{:S(2)}) copy-start(f32[8,8,128]{2,1,0:T(8,128)} %param.27) | copy-start | bytes 98308
  4.5 13.5 %all-to-all-start = ((s32[8,1,64]{2,1,0:T(1,128)}), s32[8,1,64]{2,1,0:T(1,128)S(1)}, u32[]{:S(2)}, u32[]{:S(2)}) async-start(s32[8,1,64]{2,1,0:T(1,128)} %all_to_all.9), calls=%async_computation | async-start | bytes 8192 | tf_op jit(solution)/shard_map/all_to_all | solution.py:170
  8.9 5.7 %copy-start.12 = (f32[8,8,128]{2,1,0:T(8,128)S(1)}, f32[8,8,128]{2,1,0:T(8,128)}, u32[]{:S(2)}) copy-start(f32[8,8,128]{2,1,0:T(8,128)} %param.33) | copy-start | bytes 98308
  8.9 5.7 %copy-start.13 = (f32[8,8,128]{2,1,0:T(8,128)S(1)}, f32[8,8,128]{2,1,0:T(8,128)}, u32[]{:S(2)}) copy-start(f32[8,8,128]{2,1,0:T(8,128)} %param.32) | copy-start | bytes 98308
  8.9 5.5 %copy-start.17 = (s32[256]{0:T(256)S(1)}, s32[256]{0:T(256)}, u32[]{:S(2)}) copy-start(s32[256]{0:T(256)} %param.41) | copy-start | bytes 3076
  8.9 5.5 %copy-start.18 = (f32[64]{0:T(128)S(1)}, f32[64]{0:T(128)}, u32[]{:S(2)}) copy-start(f32[64]{0:T(128)} %param.38) | copy-start | bytes 772
  8.9 44.7 %collective-permute-start.1 = (f32[2,8,4,128]{3,2,1,0:T(4,128)S(1)}, f32[2,8,4,128]{3,2,1,0:T(4,128)S(1)}, u32[]{:S(2)}, u32[]{:S(2)}) collective-permute-start(f32[2,8,4,128]{3,2,1,0:T(4,128)S(1)} %get-tuple-element.85), channel_id=1, source_target_pairs={{0,8},{8,16},{16,24},{1,9},{9,17},{17,25},{2,10},{10,18},{18,26},{... | collective-permute-start | bytes 98312 | tf_op jit(solution)/shard_map/ppermute | solution.py:15
  12.5 41.1 %collective-permute-start = (f32[2,8,4,128]{3,2,1,0:T(4,128)S(1)}, f32[2,8,4,128]{3,2,1,0:T(4,128)S(1)}, u32[]{:S(2)}, u32[]{:S(2)}) collective-permute-start(f32[2,8,4,128]{3,2,1,0:T(4,128)S(1)} %get-tuple-element.86), channel_id=1, source_target_pairs={{8,0},{16,8},{24,16},{9,1},{17,9},{25,17},{10,2},{18,10},{26,18},{... | collective-permute-start | bytes 98312 | tf_op jit(solution)/shard_map/ppermute | solution.py:18
  14.8 0.7 copy-start.16
  18.0 8.2 %all-to-all-start.1 = ((f32[8,1,128]{2,1,0:T(1,128)}), f32[8,1,128]{2,1,0:T(1,128)S(1)}, u32[]{:S(2)}, u32[]{:S(2)}) async-start(f32[8,1,128]{2,1,0:T(1,128)} %reshape.234), calls=%async_computation.1 | async-start | bytes 8192 | tf_op jit(solution)/shard_map/all_to_all | solution.py:169
  53.8 4.0 %collective-permute-start.3 = (f32[2,8,16,4]{3,2,1,0:T(8,128)S(1)}, f32[2,8,16,4]{3,2,1,0:T(8,128)S(1)}, u32[]{:S(2)}, u32[]{:S(2)}) collective-permute-start(f32[2,8,16,4]{3,2,1,0:T(8,128)S(1)} %get-tuple-element.72), channel_id=1, source_target_pairs={{0,4},{1,5},{2,6},{3,7},{8,12},{9,13},{10,14},{11,15},{16,20},{17,... | collective-permute-start | bytes 12296 | tf_op jit(solution)/shard_map/ppermute | solution.py:15
  55.9 5.7 %collective-permute-start.2 = (f32[2,8,16,4]{3,2,1,0:T(8,128)S(1)}, f32[2,8,16,4]{3,2,1,0:T(8,128)S(1)}, u32[]{:S(2)}, u32[]{:S(2)}) collective-permute-start(f32[2,8,16,4]{3,2,1,0:T(8,128)S(1)} %get-tuple-element.73), channel_id=1, source_target_pairs={{4,0},{5,1},{6,2},{7,3},{12,8},{13,9},{14,10},{15,11},{20,16},{21,... | collective-permute-start | bytes 12296 | tf_op jit(solution)/shard_map/ppermute | solution.py:18
  61.9 6.0 %collective-permute-start.4 = (f32[2,4,16,136]{3,2,1,0:T(8,128)S(1)}, f32[2,4,16,136]{3,2,1,0:T(8,128)S(1)}, u32[]{:S(2)}, u32[]{:S(2)}) collective-permute-start(f32[2,4,16,136]{3,2,1,0:T(8,128)S(1)} %get-tuple-element.60), channel_id=1, source_target_pairs={{1,0},{2,1},{3,2},{5,4},{6,5},{7,6},{9,8},{10,9},{11,10},{13,12},{... | collective-permute-start | bytes 208904 | tf_op jit(solution)/shard_map/ppermute | solution.py:18
  63.9 6.2 %collective-permute-start.5 = (f32[2,4,16,136]{3,2,1,0:T(8,128)S(1)}, f32[2,4,16,136]{3,2,1,0:T(8,128)S(1)}, u32[]{:S(2)}, u32[]{:S(2)}) collective-permute-start(f32[2,4,16,136]{3,2,1,0:T(8,128)S(1)} %get-tuple-element.61), channel_id=1, source_target_pairs={{0,1},{1,2},{2,3},{4,5},{5,6},{6,7},{8,9},{9,10},{10,11},{12,13},{... | collective-permute-start | bytes 208904 | tf_op jit(solution)/shard_map/ppermute | solution.py:15
  70.9 0.8 copy-start.5
  70.9 0.8 copy-start.6
  70.9 0.8 copy-start.7
  71.0 0.8 copy-start.8
  71.0 0.8 copy-start.9
  71.0 0.8 copy-start.14
  71.0 0.8 copy-start.15
  71.9 36.0 %copy-start.1 = (f32[8,8,128]{2,1,0:T(8,128)}, f32[8,8,128]{2,1,0:T(8,128)S(1)}, u32[]{:S(2)}) copy-start(f32[8,8,128]{2,1,0:T(8,128)S(1)} %get-tuple-element.94) | copy-start | bytes 98308
  71.9 36.0 %copy-start.2 = (f32[8,8,128]{2,1,0:T(8,128)}, f32[8,8,128]{2,1,0:T(8,128)S(1)}, u32[]{:S(2)}) copy-start(f32[8,8,128]{2,1,0:T(8,128)S(1)} %get-tuple-element.95) | copy-start | bytes 98308
  71.9 12.9 %collective-permute-start.7 = (f32[2,8,4,128]{3,2,1,0:T(4,128)S(1)}, f32[2,8,4,128]{3,2,1,0:T(4,128)S(1)}, u32[]{:S(2)}, u32[]{:S(2)}) collective-permute-start(f32[2,8,4,128]{3,2,1,0:T(4,128)S(1)} %get-tuple-element.76), channel_id=1, source_target_pairs={{0,8},{8,16},{16,24},{1,9},{9,17},{17,25},{2,10},{10,18},{18,26},{... | collective-permute-start | bytes 98312 | tf_op jit(solution)/shard_map/ppermute | solution.py:15
  82.9 5.2 %collective-permute-start.6 = (f32[2,8,4,128]{3,2,1,0:T(4,128)S(1)}, f32[2,8,4,128]{3,2,1,0:T(4,128)S(1)}, u32[]{:S(2)}, u32[]{:S(2)}) collective-permute-start(f32[2,8,4,128]{3,2,1,0:T(4,128)S(1)} %get-tuple-element.77), channel_id=1, source_target_pairs={{8,0},{16,8},{24,16},{9,1},{17,9},{25,17},{10,2},{18,10},{26,18},{... | collective-permute-start | bytes 98312 | tf_op jit(solution)/shard_map/ppermute | solution.py:18
  88.2 3.2 %collective-permute-start.9 = (f32[2,8,16,4]{3,2,1,0:T(8,128)S(1)}, f32[2,8,16,4]{3,2,1,0:T(8,128)S(1)}, u32[]{:S(2)}, u32[]{:S(2)}) collective-permute-start(f32[2,8,16,4]{3,2,1,0:T(8,128)S(1)} %get-tuple-element.68), channel_id=1, source_target_pairs={{0,4},{1,5},{2,6},{3,7},{8,12},{9,13},{10,14},{11,15},{16,20},{17,... | collective-permute-start | bytes 12296 | tf_op jit(solution)/shard_map/ppermute | solution.py:15
  89.5 5.7 %collective-permute-start.8 = (f32[2,8,16,4]{3,2,1,0:T(8,128)S(1)}, f32[2,8,16,4]{3,2,1,0:T(8,128)S(1)}, u32[]{:S(2)}, u32[]{:S(2)}) collective-permute-start(f32[2,8,16,4]{3,2,1,0:T(8,128)S(1)} %get-tuple-element.69), channel_id=1, source_target_pairs={{4,0},{5,1},{6,2},{7,3},{12,8},{13,9},{14,10},{15,11},{20,16},{21,... | collective-permute-start | bytes 12296 | tf_op jit(solution)/shard_map/ppermute | solution.py:18
  95.5 6.8 %collective-permute-start.10 = (f32[2,4,16,136]{3,2,1,0:T(8,128)S(1)}, f32[2,4,16,136]{3,2,1,0:T(8,128)S(1)}, u32[]{:S(2)}, u32[]{:S(2)}) collective-permute-start(f32[2,4,16,136]{3,2,1,0:T(8,128)S(1)} %get-tuple-element.58), channel_id=1, source_target_pairs={{1,0},{2,1},{3,2},{5,4},{6,5},{7,6},{9,8},{10,9},{11,10},{13,12},{... | collective-permute-start | bytes 208904 | tf_op jit(solution)/shard_map/ppermute | solution.py:18
  99.2 7.3 %collective-permute-start.11 = (f32[2,4,16,136]{3,2,1,0:T(8,128)S(1)}, f32[2,4,16,136]{3,2,1,0:T(8,128)S(1)}, u32[]{:S(2)}, u32[]{:S(2)}) collective-permute-start(f32[2,4,16,136]{3,2,1,0:T(8,128)S(1)} %get-tuple-element.59), channel_id=1, source_target_pairs={{0,1},{1,2},{2,3},{4,5},{5,6},{6,7},{8,9},{9,10},{10,11},{12,13},{... | collective-permute-start | bytes 208904 | tf_op jit(solution)/shard_map/ppermute | solution.py:15
  107.9 0.6 copy-start.10
  107.9 0.6 copy-start.11
where the time goes:
time: 109 us
  starting transfers between devices  43.9 us (40%)
  blocking collectives  23.1 us (21%)
  waiting for transfers between devices  22.7 us (21%)
  other arithmetic  9.15 us (8%)
  local copies, waits for them, and re-layouts  8.32 us (8%)
  between operations  1.24 us (1%)
    psum x1, blocking collectives, local(): planes = lax.psum(planes, 'gz')  23.1 us
    ppermute x6, starting transfers between devices, with_halo(): lax.ppermute(lax.slice_in_dim(block, block.shape[dim] - width, None, axis...  23 us
    ppermute x6, waiting for transfers between devices, with_halo(): lax.ppermute(lax.slice_in_dim(block, 0, width, axis=dim), axis, backward)  12.4 us
    ppermute x6, starting transfers between devices, with_halo(): lax.ppermute(lax.slice_in_dim(block, 0, width, axis=dim), axis, backward)  12.1 us
    ppermute x6, waiting for transfers between devices, with_halo(): lax.ppermute(lax.slice_in_dim(block, block.shape[dim] - width, None, axis...  7.67 us
    all_to_all x1, starting transfers between devices, local(): lax.all_to_all(label_buffer, ('inl', 'xl'), split_axis=0, concat_axis=0,...  4.39 us
    all_to_all x1, starting transfers between devices, local(): lax.all_to_all(float_buffer, ('inl', 'xl'), split_axis=0, concat_axis=0,...  4.3 us
    all_to_all x1, waiting for transfers between devices, local(): lax.all_to_all(float_buffer, ('inl', 'xl'), split_axis=0, concat_axis=0,...  2.63 us
  transfers between devices with their start and end apart: 14, of which 10 were waited for; matrix products, arithmetic and copies ran while one was open for 8% of the time, Pallas kernels for 0%

commit v1 on v0

--- a/solution.py
+++ b/solution.py
@@ -173,7 +173,7 @@
     flat_labels = arrived_labels.reshape(-1)
     target = jnp.where(flat_labels >= 0, flat_labels, cells)
     planes = jnp.zeros((steps, cells), jnp.float32).at[:, target].add(amplitude.T, mode="drop")
-    planes = lax.psum(planes, "gz")
+    planes = jnp.sum(lax.all_gather(planes, "gz"), axis=0)
     surface_flag = jnp.where(lax.axis_index("gz") == 0, 1.0, 0.0).astype(jnp.float32)
     planes = planes.reshape(steps, inline_cells, cross_cells) * surface_flag
     fields = (courant_square, thomsen_epsilon, thomsen_delta, shear_ratio, damping)

time: 109 us -> 92.6 us (0.85)
  blocking collectives: 23.1 us -> 8.74 us
  starting transfers between devices: 43.9 us -> 41.9 us
    psum x1 -> x0, blocking collectives: 23.1 us -> none  [local(): planes = lax.psum(planes, 'gz')]
    all_gather x0 -> x1, blocking collectives: none -> 8.74 us  [local(): planes = jnp.sum(lax.all_gather(planes, 'gz'), axis=0)]
    ppermute x6, starting transfers between devices: 23 us -> 20.9 us  [with_halo(): lax.ppermute(lax.slice_in_dim(block, block.shape[dim] - width, None, axis...]
    unnamed x40 -> x42, local copies, waits for them, and re-layouts: 2.27 us -> 2.69 us
  transfers between devices with their start and end apart: 14 -> 14, of which waited for: 10 -> 10; matrix products, arithmetic and copies ran while one was open for 8% -> 10% of each run, Pallas kernels for 0% -> 0%
where the time goes in v1:
time: 92.6 us; the launch traced here: 92 us
  starting transfers between devices  41.9 us (45%)
  waiting for transfers between devices  21.9 us (24%)
  other arithmetic  9.16 us (10%)
  local copies, waits for them, and re-layouts  8.74 us (9%)
  blocking collectives  8.74 us (9%)
  between operations  1.24 us (1%)
    ppermute x6, starting transfers between devices, with_halo(): lax.ppermute(lax.slice_in_dim(block, block.shape[dim] - width, None, axis...  20.9 us
    ppermute x6, waiting for transfers between devices, with_halo(): lax.ppermute(lax.slice_in_dim(block, 0, width, axis=dim), axis, backward)  12.7 us
    ppermute x6, starting transfers between devices, with_halo(): lax.ppermute(lax.slice_in_dim(block, 0, width, axis=dim), axis, backward)  12.3 us
    all_gather x1, blocking collectives, local(): planes = jnp.sum(lax.all_gather(planes, 'gz'), axis=0)  8.74 us
    ppermute x6, waiting for transfers between devices, with_halo(): lax.ppermute(lax.slice_in_dim(block, block.shape[dim] - width, None, axis...  6.63 us
    all_to_all x1, starting transfers between devices, local(): lax.all_to_all(label_buffer, ('inl', 'xl'), split_axis=0, concat_axis=0,...  4.39 us
    all_to_all x1, starting transfers between devices, local(): lax.all_to_all(float_buffer, ('inl', 'xl'), split_axis=0, concat_axis=0,...  4.3 us
    unnamed x42, local copies, waits for them, and re-layouts  2.69 us
  transfers between devices with their start and end apart: 14, of which 10 were waited for; matrix products, arithmetic and copies ran while one was open for 10% of the time, Pallas kernels for 0%

profile of v1, /device:TPU:17, one launch (start us, length us, event | category | flops | bytes accessed | tf_op | source)
XLA Modules:
  0.0 92.0 jit_solution(13974730886528725347)
XLA Ops:
  0.6 0.7 fusion.178
  1.4 0.6 reduce-window.6
  2.4 1.4 %scatter_custom_fusion = s32[512]{0:T(512)S(1)} fusion(s32[256]{0:T(256)S(1)} %compare_select_fusion.2, s32[256]{0:T(256)S(1)} %get-tuple-element.96, s32[]{:T(128)} %constant.177.clone.1), kind=kCustom, calls=%fused_computation.335 | custom fusion | bytes 2052 | tf_op jit(solution)/shard_map/scatter | solution.py:165
  3.8 0.7 all_to_all.9
  4.5 4.4 %all-to-all-start = ((s32[8,1,64]{2,1,0:T(1,128)}), s32[8,1,64]{2,1,0:T(1,128)S(1)}, u32[]{:S(2)}, u32[]{:S(2)}) async-start(s32[8,1,64]{2,1,0:T(1,128)} %all_to_all.9), calls=%async_computation | async-start | bytes 8192 | tf_op jit(solution)/shard_map/all_to_all | solution.py:170
  8.9 3.5 %collective-permute-start.1 = (f32[2,8,4,128]{3,2,1,0:T(4,128)S(1)}, f32[2,8,4,128]{3,2,1,0:T(4,128)S(1)}, u32[]{:S(2)}, u32[]{:S(2)}) collective-permute-start(f32[2,8,4,128]{3,2,1,0:T(4,128)S(1)} %get-tuple-element.85), channel_id=1, source_target_pairs={{0,8},{8,16},{16,24},{1,9},{9,17},{17,25},{2,10},{10,18},{18,26},{... | collective-permute-start | bytes 98312 | tf_op jit(solution)/shard_map/ppermute | solution.py:15
  12.5 1.9 %collective-permute-start = (f32[2,8,4,128]{3,2,1,0:T(4,128)S(1)}, f32[2,8,4,128]{3,2,1,0:T(4,128)S(1)}, u32[]{:S(2)}, u32[]{:S(2)}) collective-permute-start(f32[2,8,4,128]{3,2,1,0:T(4,128)S(1)} %get-tuple-element.86), channel_id=1, source_target_pairs={{8,0},{16,8},{24,16},{9,1},{17,9},{25,17},{10,2},{18,10},{26,18},{... | collective-permute-start | bytes 98312 | tf_op jit(solution)/shard_map/ppermute | solution.py:18
  14.5 0.2 fusion.187
  14.8 0.6 copy-done.16
  15.5 0.3 convolution_multiply_fusion
  15.9 1.2 %scatter_custom_fusion.1 = f32[512,2]{1,0:T(8,128)S(1)} fusion(s32[256]{0:T(256)S(1)} %compare_select_fusion.2, f32[256,2]{1,0:T(8,128)S(1)} %copy.32, f32[]{:T(128)} %constant.176.clone.1), kind=kCustom, calls=%fused_computation.67 | custom fusion | bytes 4100 | tf_op jit(solution)/shard_map/scatter | solution.py:159
  17.3 0.7 reshape.238
  18.0 4.3 %all-to-all-start.1 = ((f32[8,1,128]{2,1,0:T(1,128)}), f32[8,1,128]{2,1,0:T(1,128)S(1)}, u32[]{:S(2)}, u32[]{:S(2)}) async-start(f32[8,1,128]{2,1,0:T(1,128)} %reshape.238), calls=%async_computation.1 | async-start | bytes 8192 | tf_op jit(solution)/shard_map/all_to_all | solution.py:169
  22.3 0.5 broadcast.341
  22.8 0.7 reduce.18
  23.6 2.6 %all-to-all-done.1 = f32[8,1,128]{2,1,0:T(1,128)S(1)} async-done(((f32[8,1,128]{2,1,0:T(1,128)}), f32[8,1,128]{2,1,0:T(1,128)S(1)}, u32[]{:S(2)}, u32[]{:S(2)}) %all-to-all-start.1) | async-done | bytes 4128 | tf_op jit(solution)/shard_map/all_to_all | solution.py:169
  26.2 0.5 broadcast.390
  26.7 0.7 reduce.19
  27.6 2.4 %scatter_custom_fusion.2 = f32[2,1024]{0,1:T(8,128)S(1)} fusion(s32[512]{0:T(512)S(1)} %bitcast.141, f32[512,2]{1,0:T(8,128)S(1)} %bitcast.137, f32[]{:T(128)} %constant.176.clone.1), kind=kCustom, calls=%fused_computation.37 | custom fusion | flops 1024 | bytes 8196 | tf_op jit(solution)/shard_map/scatter-add | solution.py:175
  30.2 8.7 %all-gather.1 = f32[4,2,1024]{2,1,0:T(2,128)S(1)} all-gather(f32[1,2,1024]{2,1,0:T(2,128)S(1)} %copy.36), channel_id=2, replica_groups=mesh['inl'=4,'xl'=2,'gz'=4] {'gz'}, dimensions={0}, use_global_device_ids=true | all-gather | bytes 40960 | tf_op jit(solution)/shard_map/all_gather | solution.py:176
  39.2 0.5 slice_reduce_fusion
  39.9 2.2 %collective-permute-start.3 = (f32[2,8,16,4]{3,2,1,0:T(8,128)S(1)}, f32[2,8,16,4]{3,2,1,0:T(8,128)S(1)}, u32[]{:S(2)}, u32[]{:S(2)}) collective-permute-start(f32[2,8,16,4]{3,2,1,0:T(8,128)S(1)} %get-tuple-element.72), channel_id=1, source_target_pairs={{0,4},{1,5},{2,6},{3,7},{8,12},{9,13},{10,14},{11,15},{16,20},{17,... | collective-permute-start | bytes 12296 | tf_op jit(solution)/shard_map/ppermute | solution.py:15
  42.1 1.3 %collective-permute-start.2 = (f32[2,8,16,4]{3,2,1,0:T(8,128)S(1)}, f32[2,8,16,4]{3,2,1,0:T(8,128)S(1)}, u32[]{:S(2)}, u32[]{:S(2)}) collective-permute-start(f32[2,8,16,4]{3,2,1,0:T(8,128)S(1)} %get-tuple-element.73), channel_id=1, source_target_pairs={{4,0},{5,1},{6,2},{7,3},{12,8},{13,9},{14,10},{15,11},{20,16},{21,... | collective-permute-start | bytes 12296 | tf_op jit(solution)/shard_map/ppermute | solution.py:18
  43.4 0.6 collective-permute-done.3
  44.0 3.8 %collective-permute-done.2 = f32[2,8,16,4]{3,2,1,0:T(8,128)S(1)} collective-permute-done((f32[2,8,16,4]{3,2,1,0:T(8,128)S(1)}, f32[2,8,16,4]{3,2,1,0:T(8,128)S(1)}, u32[]{:S(2)}, u32[]{:S(2)}) %collective-permute-start.2) | collective-permute-done | bytes 4128 | tf_op jit(solution)/shard_map/ppermute | solution.py:18
  47.8 0.2 pad_maximum_fusion.3
  48.1 3.8 %collective-permute-start.4 = (f32[2,4,16,136]{3,2,1,0:T(8,128)S(1)}, f32[2,4,16,136]{3,2,1,0:T(8,128)S(1)}, u32[]{:S(2)}, u32[]{:S(2)}) collective-permute-start(f32[2,4,16,136]{3,2,1,0:T(8,128)S(1)} %get-tuple-element.60), channel_id=1, source_target_pairs={{1,0},{2,1},{3,2},{5,4},{6,5},{7,6},{9,8},{10,9},{11,10},{13,12},{... | collective-permute-start | bytes 208904 | tf_op jit(solution)/shard_map/ppermute | solution.py:18
  51.9 2.2 %collective-permute-start.5 = (f32[2,4,16,136]{3,2,1,0:T(8,128)S(1)}, f32[2,4,16,136]{3,2,1,0:T(8,128)S(1)}, u32[]{:S(2)}, u32[]{:S(2)}) collective-permute-start(f32[2,4,16,136]{3,2,1,0:T(8,128)S(1)} %get-tuple-element.61), channel_id=1, source_target_pairs={{0,1},{1,2},{2,3},{4,5},{5,6},{6,7},{8,9},{9,10},{10,11},{12,13},{... | collective-permute-start | bytes 208904 | tf_op jit(solution)/shard_map/ppermute | solution.py:15
  54.5 3.1 %collective-permute-done.5 = f32[2,4,16,136]{3,2,1,0:T(8,128)S(1)} collective-permute-done((f32[2,4,16,136]{3,2,1,0:T(8,128)S(1)}, f32[2,4,16,136]{3,2,1,0:T(8,128)S(1)}, u32[]{:S(2)}, u32[]{:S(2)}) %collective-permute-start.5) | collective-permute-done | bytes 69664 | tf_op jit(solution)/shard_map/ppermute | solution.py:15
  57.6 0.2 pad_maximum_fusion
  57.8 0.3 fusion.24
  58.4 0.6 add_subtract_fusion.1
  59.3 8.5 %collective-permute-start.7 = (f32[2,8,4,128]{3,2,1,0:T(4,128)S(1)}, f32[2,8,4,128]{3,2,1,0:T(4,128)S(1)}, u32[]{:S(2)}, u32[]{:S(2)}) collective-permute-start(f32[2,8,4,128]{3,2,1,0:T(4,128)S(1)} %get-tuple-element.76), channel_id=1, source_target_pairs={{0,8},{8,16},{16,24},{1,9},{9,17},{17,25},{2,10},{10,18},{18,26},{... | collective-permute-start | bytes 98312 | tf_op jit(solution)/shard_map/ppermute | solution.py:15
  67.8 1.9 %collective-permute-start.6 = (f32[2,8,4,128]{3,2,1,0:T(4,128)S(1)}, f32[2,8,4,128]{3,2,1,0:T(4,128)S(1)}, u32[]{:S(2)}, u32[]{:S(2)}) collective-permute-start(f32[2,8,4,128]{3,2,1,0:T(4,128)S(1)} %get-tuple-element.77), channel_id=1, source_target_pairs={{8,0},{16,8},{24,16},{9,1},{17,9},{25,17},{10,2},{18,10},{26,18},{... | collective-permute-start | bytes 98312 | tf_op jit(solution)/shard_map/ppermute | solution.py:18
  69.8 3.3 %collective-permute-done.6 = f32[2,8,4,128]{3,2,1,0:T(4,128)S(1)} collective-permute-done((f32[2,8,4,128]{3,2,1,0:T(4,128)S(1)}, f32[2,8,4,128]{3,2,1,0:T(4,128)S(1)}, u32[]{:S(2)}, u32[]{:S(2)}) %collective-permute-start.6) | collective-permute-done | bytes 32800 | tf_op jit(solution)/shard_map/ppermute | solution.py:18
  73.2 1.3 %collective-permute-start.9 = (f32[2,8,16,4]{3,2,1,0:T(8,128)S(1)}, f32[2,8,16,4]{3,2,1,0:T(8,128)S(1)}, u32[]{:S(2)}, u32[]{:S(2)}) collective-permute-start(f32[2,8,16,4]{3,2,1,0:T(8,128)S(1)} %get-tuple-element.68), channel_id=1, source_target_pairs={{0,4},{1,5},{2,6},{3,7},{8,12},{9,13},{10,14},{11,15},{16,20},{17,... | collective-permute-start | bytes 12296 | tf_op jit(solution)/shard_map/ppermute | solution.py:15
  74.5 1.3 %collective-permute-start.8 = (f32[2,8,16,4]{3,2,1,0:T(8,128)S(1)}, f32[2,8,16,4]{3,2,1,0:T(8,128)S(1)}, u32[]{:S(2)}, u32[]{:S(2)}) collective-permute-start(f32[2,8,16,4]{3,2,1,0:T(8,128)S(1)} %get-tuple-element.69), channel_id=1, source_target_pairs={{4,0},{5,1},{6,2},{7,3},{12,8},{13,9},{14,10},{15,11},{20,16},{21,... | collective-permute-start | bytes 12296 | tf_op jit(solution)/shard_map/ppermute | solution.py:18
  75.8 0.6 collective-permute-done.9
  76.4 3.8 %collective-permute-done.8 = f32[2,8,16,4]{3,2,1,0:T(8,128)S(1)} collective-permute-done((f32[2,8,16,4]{3,2,1,0:T(8,128)S(1)}, f32[2,8,16,4]{3,2,1,0:T(8,128)S(1)}, u32[]{:S(2)}, u32[]{:S(2)}) %collective-permute-start.8) | collective-permute-done | bytes 4128 | tf_op jit(solution)/shard_map/ppermute | solution.py:18
  80.2 0.2 pad_maximum_fusion.5
  80.5 2.1 %collective-permute-start.10 = (f32[2,4,16,136]{3,2,1,0:T(8,128)S(1)}, f32[2,4,16,136]{3,2,1,0:T(8,128)S(1)}, u32[]{:S(2)}, u32[]{:S(2)}) collective-permute-start(f32[2,4,16,136]{3,2,1,0:T(8,128)S(1)} %get-tuple-element.58), channel_id=1, source_target_pairs={{1,0},{2,1},{3,2},{5,4},{6,5},{7,6},{9,8},{10,9},{11,10},{13,12},{... | collective-permute-start | bytes 208904 | tf_op jit(solution)/shard_map/ppermute | solution.py:18
  82.6 3.2 %collective-permute-start.11 = (f32[2,4,16,136]{3,2,1,0:T(8,128)S(1)}, f32[2,4,16,136]{3,2,1,0:T(8,128)S(1)}, u32[]{:S(2)}, u32[]{:S(2)}) collective-permute-start(f32[2,4,16,136]{3,2,1,0:T(8,128)S(1)} %get-tuple-element.59), channel_id=1, source_target_pairs={{0,1},{1,2},{2,3},{4,5},{5,6},{6,7},{8,9},{9,10},{10,11},{12,13},{... | collective-permute-start | bytes 208904 | tf_op jit(solution)/shard_map/ppermute | solution.py:15
  86.0 1.6 %collective-permute-done.10 = f32[2,4,16,136]{3,2,1,0:T(8,128)S(1)} collective-permute-done((f32[2,4,16,136]{3,2,1,0:T(8,128)S(1)}, f32[2,4,16,136]{3,2,1,0:T(8,128)S(1)}, u32[]{:S(2)}, u32[]{:S(2)}) %collective-permute-start.10) | collective-permute-done | bytes 69664 | tf_op jit(solution)/shard_map/ppermute | solution.py:18
  87.6 2.4 %collective-permute-done.11 = f32[2,4,16,136]{3,2,1,0:T(8,128)S(1)} collective-permute-done((f32[2,4,16,136]{3,2,1,0:T(8,128)S(1)}, f32[2,4,16,136]{3,2,1,0:T(8,128)S(1)}, u32[]{:S(2)}, u32[]{:S(2)}) %collective-permute-start.11) | collective-permute-done | bytes 69664 | tf_op jit(solution)/shard_map/ppermute | solution.py:15
  89.9 0.2 pad_maximum_fusion.1
  90.2 0.3 fusion.17
  90.7 0.6 add_subtract_fusion
  91.4 0.6 copy-done.10
  (77 shorter events, 3.3 us)
Async XLA Ops:
  0.6 14.2 %copy-start = (f32[256,256]{1,0:T(8,128)S(1)}, f32[256,256]{1,0:T(8,128)}, u32[]{:S(2)}) copy-start(f32[256,256]{1,0:T(8,128)} %param.36) | copy-start | bytes 786436
  1.4 7.4 %copy-start.3 = (f32[8,8,128]{2,1,0:T(8,128)S(1)}, f32[8,8,128]{2,1,0:T(8,128)}, u32[]{:S(2)}) copy-start(f32[8,8,128]{2,1,0:T(8,128)} %param.25) | copy-start | bytes 98308
  1.4 7.4 %copy-start.4 = (f32[8,8,128]{2,1,0:T(8,128)S(1)}, f32[8,8,128]{2,1,0:T(8,128)}, u32[]{:S(2)}) copy-start(f32[8,8,128]{2,1,0:T(8,128)} %param.27) | copy-start | bytes 98308
  4.5 13.5 %all-to-all-start = ((s32[8,1,64]{2,1,0:T(1,128)}), s32[8,1,64]{2,1,0:T(1,128)S(1)}, u32[]{:S(2)}, u32[]{:S(2)}) async-start(s32[8,1,64]{2,1,0:T(1,128)} %all_to_all.9), calls=%async_computation | async-start | bytes 8192 | tf_op jit(solution)/shard_map/all_to_all | solution.py:170
  8.9 5.7 %copy-start.12 = (f32[8,8,128]{2,1,0:T(8,128)S(1)}, f32[8,8,128]{2,1,0:T(8,128)}, u32[]{:S(2)}) copy-start(f32[8,8,128]{2,1,0:T(8,128)} %param.33) | copy-start | bytes 98308
  8.9 5.7 %copy-start.13 = (f32[8,8,128]{2,1,0:T(8,128)S(1)}, f32[8,8,128]{2,1,0:T(8,128)}, u32[]{:S(2)}) copy-start(f32[8,8,128]{2,1,0:T(8,128)} %param.32) | copy-start | bytes 98308
  8.9 5.5 %copy-start.17 = (s32[256]{0:T(256)S(1)}, s32[256]{0:T(256)}, u32[]{:S(2)}) copy-start(s32[256]{0:T(256)} %param.41) | copy-start | bytes 3076
  8.9 5.5 %copy-start.18 = (f32[64]{0:T(128)S(1)}, f32[64]{0:T(128)}, u32[]{:S(2)}) copy-start(f32[64]{0:T(128)} %param.38) | copy-start | bytes 772
  8.9 30.8 %collective-permute-start.1 = (f32[2,8,4,128]{3,2,1,0:T(4,128)S(1)}, f32[2,8,4,128]{3,2,1,0:T(4,128)S(1)}, u32[]{:S(2)}, u32[]{:S(2)}) collective-permute-start(f32[2,8,4,128]{3,2,1,0:T(4,128)S(1)} %get-tuple-element.85), channel_id=1, source_target_pairs={{0,8},{8,16},{16,24},{1,9},{9,17},{17,25},{2,10},{10,18},{18,26},{... | collective-permute-start | bytes 98312 | tf_op jit(solution)/shard_map/ppermute | solution.py:15
  12.5 27.3 %collective-permute-start = (f32[2,8,4,128]{3,2,1,0:T(4,128)S(1)}, f32[2,8,4,128]{3,2,1,0:T(4,128)S(1)}, u32[]{:S(2)}, u32[]{:S(2)}) collective-permute-start(f32[2,8,4,128]{3,2,1,0:T(4,128)S(1)} %get-tuple-element.86), channel_id=1, source_target_pairs={{8,0},{16,8},{24,16},{9,1},{17,9},{25,17},{10,2},{18,10},{26,18},{... | collective-permute-start | bytes 98312 | tf_op jit(solution)/shard_map/ppermute | solution.py:18
  14.8 0.7 copy-start.16
  18.0 8.2 %all-to-all-start.1 = ((f32[8,1,128]{2,1,0:T(1,128)}), f32[8,1,128]{2,1,0:T(1,128)S(1)}, u32[]{:S(2)}, u32[]{:S(2)}) async-start(f32[8,1,128]{2,1,0:T(1,128)} %reshape.238), calls=%async_computation.1 | async-start | bytes 8192 | tf_op jit(solution)/shard_map/all_to_all | solution.py:169
  39.9 4.1 %collective-permute-start.3 = (f32[2,8,16,4]{3,2,1,0:T(8,128)S(1)}, f32[2,8,16,4]{3,2,1,0:T(8,128)S(1)}, u32[]{:S(2)}, u32[]{:S(2)}) collective-permute-start(f32[2,8,16,4]{3,2,1,0:T(8,128)S(1)} %get-tuple-element.72), channel_id=1, source_target_pairs={{0,4},{1,5},{2,6},{3,7},{8,12},{9,13},{10,14},{11,15},{16,20},{17,... | collective-permute-start | bytes 12296 | tf_op jit(solution)/shard_map/ppermute | solution.py:15
  42.1 5.7 %collective-permute-start.2 = (f32[2,8,16,4]{3,2,1,0:T(8,128)S(1)}, f32[2,8,16,4]{3,2,1,0:T(8,128)S(1)}, u32[]{:S(2)}, u32[]{:S(2)}) collective-permute-start(f32[2,8,16,4]{3,2,1,0:T(8,128)S(1)} %get-tuple-element.73), channel_id=1, source_target_pairs={{4,0},{5,1},{6,2},{7,3},{12,8},{13,9},{14,10},{15,11},{20,16},{21,... | collective-permute-start | bytes 12296 | tf_op jit(solution)/shard_map/ppermute | solution.py:18
  48.1 6.4 %collective-permute-start.4 = (f32[2,4,16,136]{3,2,1,0:T(8,128)S(1)}, f32[2,4,16,136]{3,2,1,0:T(8,128)S(1)}, u32[]{:S(2)}, u32[]{:S(2)}) collective-permute-start(f32[2,4,16,136]{3,2,1,0:T(8,128)S(1)} %get-tuple-element.60), channel_id=1, source_target_pairs={{1,0},{2,1},{3,2},{5,4},{6,5},{7,6},{9,8},{10,9},{11,10},{13,12},{... | collective-permute-start | bytes 208904 | tf_op jit(solution)/shard_map/ppermute | solution.py:18
  51.9 5.7 %collective-permute-start.5 = (f32[2,4,16,136]{3,2,1,0:T(8,128)S(1)}, f32[2,4,16,136]{3,2,1,0:T(8,128)S(1)}, u32[]{:S(2)}, u32[]{:S(2)}) collective-permute-start(f32[2,4,16,136]{3,2,1,0:T(8,128)S(1)} %get-tuple-element.61), channel_id=1, source_target_pairs={{0,1},{1,2},{2,3},{4,5},{5,6},{6,7},{8,9},{9,10},{10,11},{12,13},{... | collective-permute-start | bytes 208904 | tf_op jit(solution)/shard_map/ppermute | solution.py:15
  58.3 0.8 copy-start.5
  58.4 0.8 copy-start.6
  58.4 0.8 copy-start.7
  58.4 0.8 copy-start.8
  58.4 0.8 copy-start.9
  58.4 0.8 copy-start.14
  58.4 0.8 copy-start.15
  59.3 32.0 %copy-start.1 = (f32[8,8,128]{2,1,0:T(8,128)}, f32[8,8,128]{2,1,0:T(8,128)S(1)}, u32[]{:S(2)}) copy-start(f32[8,8,128]{2,1,0:T(8,128)S(1)} %get-tuple-element.94) | copy-start | bytes 98308
  59.3 32.0 %copy-start.2 = (f32[8,8,128]{2,1,0:T(8,128)}, f32[8,8,128]{2,1,0:T(8,128)S(1)}, u32[]{:S(2)}) copy-start(f32[8,8,128]{2,1,0:T(8,128)S(1)} %get-tuple-element.95) | copy-start | bytes 98308
  59.3 10.4 %collective-permute-start.7 = (f32[2,8,4,128]{3,2,1,0:T(4,128)S(1)}, f32[2,8,4,128]{3,2,1,0:T(4,128)S(1)}, u32[]{:S(2)}, u32[]{:S(2)}) collective-permute-start(f32[2,8,4,128]{3,2,1,0:T(4,128)S(1)} %get-tuple-element.76), channel_id=1, source_target_pairs={{0,8},{8,16},{16,24},{1,9},{9,17},{17,25},{2,10},{10,18},{18,26},{... | collective-permute-start | bytes 98312 | tf_op jit(solution)/shard_map/ppermute | solution.py:15
  67.8 5.2 %collective-permute-start.6 = (f32[2,8,4,128]{3,2,1,0:T(4,128)S(1)}, f32[2,8,4,128]{3,2,1,0:T(4,128)S(1)}, u32[]{:S(2)}, u32[]{:S(2)}) collective-permute-start(f32[2,8,4,128]{3,2,1,0:T(4,128)S(1)} %get-tuple-element.77), channel_id=1, source_target_pairs={{8,0},{16,8},{24,16},{9,1},{17,9},{25,17},{10,2},{18,10},{26,18},{... | collective-permute-start | bytes 98312 | tf_op jit(solution)/shard_map/ppermute | solution.py:18
  73.2 3.2 %collective-permute-start.9 = (f32[2,8,16,4]{3,2,1,0:T(8,128)S(1)}, f32[2,8,16,4]{3,2,1,0:T(8,128)S(1)}, u32[]{:S(2)}, u32[]{:S(2)}) collective-permute-start(f32[2,8,16,4]{3,2,1,0:T(8,128)S(1)} %get-tuple-element.68), channel_id=1, source_target_pairs={{0,4},{1,5},{2,6},{3,7},{8,12},{9,13},{10,14},{11,15},{16,20},{17,... | collective-permute-start | bytes 12296 | tf_op jit(solution)/shard_map/ppermute | solution.py:15
  74.5 5.7 %collective-permute-start.8 = (f32[2,8,16,4]{3,2,1,0:T(8,128)S(1)}, f32[2,8,16,4]{3,2,1,0:T(8,128)S(1)}, u32[]{:S(2)}, u32[]{:S(2)}) collective-permute-start(f32[2,8,16,4]{3,2,1,0:T(8,128)S(1)} %get-tuple-element.69), channel_id=1, source_target_pairs={{4,0},{5,1},{6,2},{7,3},{12,8},{13,9},{14,10},{15,11},{20,16},{21,... | collective-permute-start | bytes 12296 | tf_op jit(solution)/shard_map/ppermute | solution.py:18
  80.5 7.1 %collective-permute-start.10 = (f32[2,4,16,136]{3,2,1,0:T(8,128)S(1)}, f32[2,4,16,136]{3,2,1,0:T(8,128)S(1)}, u32[]{:S(2)}, u32[]{:S(2)}) collective-permute-start(f32[2,4,16,136]{3,2,1,0:T(8,128)S(1)} %get-tuple-element.58), channel_id=1, source_target_pairs={{1,0},{2,1},{3,2},{5,4},{6,5},{7,6},{9,8},{10,9},{11,10},{13,12},{... | collective-permute-start | bytes 208904 | tf_op jit(solution)/shard_map/ppermute | solution.py:18
  82.6 7.3 %collective-permute-start.11 = (f32[2,4,16,136]{3,2,1,0:T(8,128)S(1)}, f32[2,4,16,136]{3,2,1,0:T(8,128)S(1)}, u32[]{:S(2)}, u32[]{:S(2)}) collective-permute-start(f32[2,4,16,136]{3,2,1,0:T(8,128)S(1)} %get-tuple-element.59), channel_id=1, source_target_pairs={{0,1},{1,2},{2,3},{4,5},{5,6},{6,7},{8,9},{9,10},{10,11},{12,13},{... | collective-permute-start | bytes 208904 | tf_op jit(solution)/shard_map/ppermute | solution.py:15
  91.4 0.6 copy-start.10
  91.4 0.6 copy-start.11
